TPU v7x, 32 devices: a whole 2x2x4 slice. The times are simulated.
32 devices in a mesh: groups: 2 (over x), ctx: 16 (over z, y, core).
Axes of the slice: x: 2, y: 2, z: 4, core: 2. Of those that a mesh axis runs over, the one named last changes fastest.
Arguments:
- query_proj: bfloat16 [4096, 4096], P(('groups', 'ctx')), parts along dimension 0, may hold values from -6 to 6
- key_proj: bfloat16 [4096, 4096], P(('groups', 'ctx')), parts along dimension 0, may hold values from -6 to 6
- value_proj: bfloat16 [4096, 4096], P(('groups', 'ctx')), parts along dimension 0, may hold values from -6 to 6
- out_grad: bfloat16 [4096, 4096], P(('groups', 'ctx')), parts along dimension 0, may hold values from -6 to 6
- decay_rate: float32 [256, 16], replicated, may hold values from 0 to 0.034, as said below
- residue: float32 [256, 16], replicated, may hold values from -0.3 to 0.3
- group_of: int32 [4096], replicated, may hold values from 0 to 255, as said below
Outputs:
- hyena_out: bfloat16 [4096, 4096], P(('groups', 'ctx')), parts along dimension 0
- query_grad: bfloat16 [4096, 4096], P(('groups', 'ctx')), parts along dimension 0
- key_grad: bfloat16 [4096, 4096], P(('groups', 'ctx')), parts along dimension 0
- value_grad: bfloat16 [4096, 4096], P(('groups', 'ctx')), parts along dimension 0
- filter_update: float32 [512, 16], P('groups'), parts along dimension 0
There are 2 independent parts, one for each index of `groups`. A program takes and returns all parts, laid end to end along the dimension named above; an argument that names none is the same for every part. Nothing has to cross between parts.
Inputs may be any that keep to these rules, and one draw needn't show every extreme that they name: `group_of`: each of the 256 filter groups holds exactly 16 channels. `decay_rate`: positive rates.
All inputs are finite; a program needn't handle non-finite values.
Results may differ from a plain program's by a relative error of at most 0.005.
Values sent between devices are 32-bit elements; how exact they have to be, the bound alone decides.
No kernel may reach another device: no remote copies, remote signals or barrier semaphores. Data moves between devices by JAX's collectives and lax.ppermute only.
A program may use at most 192 MiB of HBM per device.

v0:
```python
import jax
import jax.numpy as jnp
from jax import lax
from jax.sharding import PartitionSpec as P


def carried_in(part, axis, combine, identity, reverse):
    count = lax.axis_size(axis)
    place = lax.axis_index(axis)
    ahead = count - 1 - place if reverse else place
    gathered = jax.tree.map(lambda a: lax.all_gather(a, axis), part)
    state = jax.tree.map(lambda a, e: jnp.zeros_like(a) + jnp.asarray(e, a.dtype), part, identity)

    def one(lap, state):
        source = count - 1 - lap if reverse else lap
        return combine(
            state, jax.tree.map(lambda a: lax.dynamic_index_in_dim(a, source, 0, False), gathered)
        )

    return lax.fori_loop(0, ahead, one, state)


def on_device(query_proj, key_proj, value_proj, out_grad, decay_rate, residue, group_of):
    high = lax.Precision.HIGHEST
    row_count, channel_count = query_proj.shape
    group_count, mode_count = decay_rate.shape
    per_group = channel_count // group_count
    order = jnp.argsort(group_of, stable=True)
    inverse = jnp.argsort(order, stable=True)
    query_f = query_proj.astype(jnp.float32)
    key_f = key_proj.astype(jnp.float32)
    value_f = value_proj.astype(jnp.float32)
    grad_f = out_grad.astype(jnp.float32)
    mixed = lax.optimization_barrier((key_f * value_f).astype(jnp.bfloat16))
    mixed_sorted = (
        jnp.take(mixed.T, order, axis=0)
        .astype(jnp.float32)
        .reshape(group_count, per_group, row_count)
    )
    upstream = grad_f * query_f
    upstream_sorted = jnp.take(upstream.T, order, axis=0).reshape(group_count, per_group, row_count)
    positions = jnp.arange(row_count, dtype=jnp.float32)
    powers = jnp.exp(-decay_rate[:, :, None] * positions[None, None, :])
    inverse_powers = jnp.exp(decay_rate[:, :, None] * positions[None, None, :])
    later_powers = powers * jnp.exp(-decay_rate)[:, :, None]
    reversed_powers = powers[:, :, ::-1]
    weighted = later_powers * residue[:, :, None]
    weighted_back = reversed_powers * residue[:, :, None]
    causal = (
        jnp.arange(row_count, dtype=jnp.int32)[:, None]
        >= jnp.arange(row_count, dtype=jnp.int32)[None, :]
    )
    toeplitz = jnp.einsum(
        "gmt,gms->gts", powers * residue[:, :, None], inverse_powers, precision=high
    )
    toeplitz = jnp.where(causal[None], toeplitz, 0.0)
    local_out = jnp.einsum("gts,gcs->gct", toeplitz, mixed_sorted, precision=high)
    local_back = jnp.einsum("gts,gct->gcs", toeplitz, upstream_sorted, precision=high)
    end_state = jnp.einsum("gms,gcs->mgc", reversed_powers, mixed_sorted, precision=high).reshape(
        mode_count, channel_count
    )
    head_term = jnp.einsum("gmt,gct->mgc", later_powers, upstream_sorted, precision=high).reshape(
        mode_count, channel_count
    )
    empty_state = jnp.zeros((mode_count, channel_count), jnp.float32)
    group_decay = jnp.exp(-decay_rate * row_count).T
    unit_decay = jnp.ones_like(group_decay)

    def chain_decays(earlier, later):
        widened = jnp.repeat(later[0], per_group, axis=1)
        return (earlier[0] * later[0], widened * earlier[1] + later[1])

    carry_pair = carried_in(
        (group_decay, end_state), "ctx", chain_decays, (unit_decay, empty_state), False
    )
    back_pair = carried_in(
        (group_decay, head_term), "ctx", chain_decays, (unit_decay, empty_state), True
    )
    carry_in = carry_pair[1]
    carry_back = back_pair[1]
    carry_grouped = carry_in.reshape(mode_count, group_count, per_group)
    back_grouped = carry_back.reshape(mode_count, group_count, per_group)
    out_sorted = local_out + jnp.einsum("gmt,mgc->gct", weighted, carry_grouped, precision=high)
    back_sorted = local_back + jnp.einsum(
        "gms,mgc->gcs", weighted_back, back_grouped, precision=high
    )
    cross = jnp.einsum("gct,gcs->gts", upstream_sorted, mixed_sorted, precision=high)
    cross = jnp.where(causal[None], cross, 0.0)
    inner = jnp.einsum("gts,gms->gmt", cross, inverse_powers, precision=high)
    local_grad = jnp.sum(inner * powers, axis=2)
    local_grad = (
        local_grad
        + jnp.sum((carry_in * head_term).reshape(mode_count, group_count, per_group), axis=2).T
    )
    filter_grad = lax.psum(local_grad, "ctx")
    filter_update = filter_grad / jnp.sqrt(jnp.mean(filter_grad * filter_grad) + 1e-06)
    filtered = jnp.take(out_sorted.reshape(channel_count, row_count), inverse, axis=0).T
    mixed_grad = jnp.take(back_sorted.reshape(channel_count, row_count), inverse, axis=0).T
    hyena_out = (query_f * filtered).astype(jnp.bfloat16)
    query_grad = (grad_f * filtered).astype(jnp.bfloat16)
    key_grad = (mixed_grad * value_f).astype(jnp.bfloat16)
    value_grad = (mixed_grad * key_f).astype(jnp.bfloat16)
    return (hyena_out, query_grad, key_grad, value_grad, filter_update)


def solution(mesh):
    placed = (
        P(("groups", "ctx"), None),
        P(("groups", "ctx"), None),
        P(("groups", "ctx"), None),
        P(("groups", "ctx"), None),
        P(),
        P(),
        P(),
    )
    return jax.shard_map(
        on_device,
        mesh=mesh,
        in_specs=placed,
        out_specs=(
            P(("groups", "ctx"), None),
            P(("groups", "ctx"), None),
            P(("groups", "ctx"), None),
            P(("groups", "ctx"), None),
            P("groups", None),
        ),
        check_vma=False,
    )
```

profile of v0, /device:TPU:0, one launch (start us, length us, event | category | flops | bytes accessed | tf_op | source)
XLA Modules:
  0.0 484.3 jit_solution(5520543099957598316)
XLA Ops:
  7.2 6.6 %sort.31 = (s32[4096]{0:T(1024)}, s32[4096]{0:T(1024)S(1)}) sort(s32[4096]{0:T(1024)} %param.19, s32[4096]{0:T(1024)S(1)} %iota.26), dimensions={0}, to_apply=%region_0.0 | sort | flops 49152 | bytes 65536 | tf_op jit(solution)/shard_map/jit(argsort)/sort | solution.py:28
  19.9 2.7 rev.3
  22.7 15.0 %gather_fusion = bf16[4096,128]{1,0:T(8,128)(2,1)} fusion(bf16[4096,128]{1,0:T(8,128)(2,1)S(1)} %bitcast.52, s32[4096]{0:T(1024)S(1)} %fusion.51), kind=kCustom, calls=%fused_computation.3 | custom fusion | bytes 2113536 | tf_op jit(solution)/shard_map/jit(_take)/gather | solution.py:36
  37.7 4.5 fusion.47
  42.2 3.0 copy.70
  45.4 5.8 %sort.32 = (s32[4096]{0:T(1024)}, s32[4096]{0:T(1024)S(1)}) sort(s32[4096]{0:T(1024)S(1)} %get-tuple-element.136, s32[4096]{0:T(1024)S(1)} %iota.27), dimensions={0}, to_apply=%region_3.4 | sort | flops 49152 | bytes 65536 | tf_op jit(solution)/shard_map/jit(argsort)/sort | solution.py:29
  54.7 26.0 %all-gather = f32[256,256]{1,0:T(8,128)} all-gather(f32[16,256]{1,0:T(8,128)S(1)} %get-tuple-element.186), channel_id=2, replica_groups=mesh['groups'=2,'ctx'=16] {'ctx'}, dimensions={0}, use_global_device_ids=true | all-gather | bytes 278528 | tf_op jit(solution)/shard_map/all_gather | solution.py:11
  81.9 28.7 %fusion.22 = f32[256,128,128]{2,1,0:T(8,128)S(1)} fusion(f32[256,16]{1,0:T(8,128)S(1)} %copy.69, f32[256,16]{1,0:T(8,128)S(1)} %copy.68, f32[256,16]{1,0:T(8,128)S(1)} %copy.67), kind=kOutput, calls=%fused_computation.38 | convolution fusion | flops 806879232 | bytes 16826368 | tf_op jit(solution)/shard_map/gmt,gms->gts/dot_general | solution.py:53
  110.6 5.7 %copy-done = f32[256,128,128]{2,1,0:T(8,128)} copy-done((f32[256,128,128]{2,1,0:T(8,128)}, f32[256,128,128]{2,1,0:T(8,128)S(1)}, u32[]{:S(2)}) %copy-start) | copy-done | bytes 16777240
  116.3 14.5 %fusion.4 = f32[256,16,128]{2,1,0:T(8,128)} fusion(f32[256,128,128]{2,1,0:T(8,128)S(1)} %fusion.22, pred[128,128]{1,0:T(8,128)(4,1)S(1)} %iota_compare_fusion, bf16[256,16,128]{2,1,0:T(8,128)(2,1)S(1)} %bitcast.59, pred[256,16]{1,0:T(8,128)(4,1)S(1)} %copy-done.17), kind=kOutput, calls=%fused_computation.12 | convolution fusion | flops 810024960 | bytes 19943424 | tf_op jit(solution)/shard_map/gts,gcs->gct/dot_general | solution.py:57
  131.7 2.9 copy.83
  134.6 5.0 %fusion.28 = f32[256,16,128]{2,1,0:T(8,128)S(1)} fusion(f32[256,16,128]{2,1,0:T(8,128)} %fusion.4, f32[16,256,16]{0,2,1:T(8,128)} %bitcast.61, f32[256,16]{1,0:T(8,128)S(1)} %copy-done.12, f32[256,16]{1,0:T(8,128)S(1)} %copy-done.10, f32[256,16]{1,0:T(8,128)S(1)} %copy.67), kind=kOutput, calls=%fused_computation.43 | convolution fusion | flops 102760448 | bytes 4505600 | tf_op jit(solution)/shard_map/gmt,mgc->gct/dot_general | solution.py:83
  139.6 15.5 %gather_fusion.1 = f32[4096,128]{1,0:T(8,128)} fusion(f32[4096,128]{1,0:T(8,128)S(1)} %bitcast.50, s32[4096]{0:T(1024)} %fusion.52), kind=kCustom, calls=%fused_computation.clone | custom fusion | bytes 4210688 | tf_op jit(solution)/shard_map/jit(_take)/gather | solution.py:97
  155.1 5.1 %fusion.16 = (bf16[128,4096]{0,1:T(8,128)(2,1)}, bf16[128,4096]{0,1:T(8,128)(2,1)}, f32[4096,128]{1,0:T(8,128)S(1)}) fusion(bf16[128,4096]{0,1:T(8,128)(2,1)} %copy.73, f32[4096,128]{1,0:T(8,128)} %gather_fusion.1, pred[4096]{0:T(1024)(128)(4,1)S(1)} %copy-done.26, bf16[128,4096]{0,1:T(8,128)(2,1)} %copy.64), kind=kLoop, calls=%fused_computation.30 | loop fusion | flops 4194304 | bytes 8392704 | tf_op jit(solution)/shard_map/convert_element_type | solution.py:100
  160.2 14.2 %gather_fusion.2 = f32[4096,128]{1,0:T(8,128)} fusion(f32[4096,128]{1,0:T(8,128)S(1)} %get-tuple-element.184, s32[4096]{0:T(1024)S(1)} %copy-done.21), kind=kCustom, calls=%fused_computation.1.clone | custom fusion | bytes 4210688 | tf_op jit(solution)/shard_map/jit(_take)/gather | solution.py:41
  174.4 3.6 broadcast_select_fusion
  178.0 5.4 %fusion.25 = f32[256,16,16]{2,1,0:T(8,128)} fusion(f32[256,16,128]{2,1,0:T(8,128)S(1)} %bitcast.53, f32[256,16]{1,0:T(8,128)S(1)} %copy-done.12, f32[256,16]{1,0:T(8,128)S(1)} %copy.67), kind=kOutput, calls=%fused_computation.42 | convolution fusion | flops 101711872 | bytes 2392064 | tf_op jit(solution)/shard_map/gmt,gct->mgc/dot_general | solution.py:62
  183.4 2.9 copy.74
  186.3 2.3 copy.79
  188.5 2.7 copy.78
  191.2 2.9 copy.76
  195.8 3.0 reshape.82
  198.8 2.2 reduce_sum.28
  201.8 13.9 %fusion.46 = f32[256,128,128]{2,1,0:T(8,128)S(1)} fusion(f32[256,16,128]{2,1,0:T(8,128)S(1)} %bitcast.54, bf16[256,16,128]{2,1,0:T(8,128)(2,1)S(1)} %bitcast.60, pred[256,16]{1,0:T(8,128)(4,1)S(1)} %copy-done.18), kind=kOutput, calls=%fused_computation.57 | convolution fusion | flops 805830656 | bytes 19927040 | tf_op jit(solution)/shard_map/gct,gcs->gts/dot_general | solution.py:87
  215.7 26.9 %multiply_reduce_fusion = f32[256,16]{1,0:T(8,128)S(1)} fusion(f32[256,16]{1,0:T(8,128)S(1)} %copy.67, f32[256,128,128]{2,1,0:T(8,128)S(1)} %fusion.46, pred[128,128]{1,0:T(8,128)(4,1)S(1)} %iota_compare_fusion, f32[256,16]{1,0:T(8,128)S(1)} %copy-done.8), kind=kOutput, calls=%fused_computation.32 | convolution fusion | flops 811593728 | bytes 16842752 | tf_op jit(solution)/shard_map/gts,gms->gmt/dot_general | solution.py:89
  242.6 127.4 %psum.7 = f32[256,16]{1,0:T(8,128)S(1)} all-reduce(f32[256,16]{1,0:T(8,128)S(1)} %bitcast_add_fusion.2), channel_id=1, replica_groups=mesh['groups'=2,'ctx'=16] {'ctx'}, use_global_device_ids=true, to_apply=%region_8.10 | all-reduce | flops 4096 | bytes 32768 | tf_op jit(solution)/shard_map/psum | solution.py:95
  372.1 17.6 %fusion.2 = f32[256,16,128]{2,1,0:T(8,128)} fusion(f32[256,16,128]{2,1,0:T(8,128)S(1)} %bitcast.55, f32[256,128,128]{2,1,0:T(8,128)} %copy-done, pred[128,128]{1,0:T(8,128)(4,1)S(1)} %iota_compare_fusion), kind=kOutput, calls=%fused_computation.10 | convolution fusion | flops 809500672 | bytes 20987904 | tf_op jit(solution)/shard_map/gts,gct->gcs/dot_general | solution.py:58
  389.7 59.8 %while.27 = (s32[]{:T(128)}, f32[16,4096]{1,0:T(8,128)S(1)}, s32[]{:T(128)}, f32[16,16,256]{2,1,0:T(8,128)}, f32[16,16,4096]{2,1,0:T(8,128)}, /*index=5*/s32[]{:T(128)}, s32[]{:T(128)}, s32[]{:T(128)}, s32[]{:T(128)}) while((s32[]{:T(128)}, f32[16,4096]{1,0:T(8,128)S(1)}, s32[]{:T(128)}, f32[16,16,256]{2,1,0:T(8,128)}, ...), condition=%wide.region_5.7_spmd, body=%wide.region_4.6_spmd.sunk | while | flops 131078 | bytes 1884315 | solution.py:20
  449.5 1.9 copy.84
  451.4 5.1 %fusion.31 = f32[256,16,128]{2,1,0:T(8,128)S(1)} fusion(f32[256,16,128]{2,1,0:T(8,128)} %fusion.2, f32[16,256,16]{0,2,1:T(8,128)} %bitcast.63, f32[256,16,128]{2,1,0:T(8,128)} %copy-done.1, f32[256,16]{1,0:T(8,128)S(1)} %copy-done.11), kind=kOutput, calls=%fused_computation.44 | convolution fusion | flops 101711872 | bytes 6569984 | tf_op jit(solution)/shard_map/gms,mgc->gcs/dot_general | solution.py:84
  456.6 14.2 %gather_fusion.3 = f32[4096,128]{1,0:T(8,128)} fusion(f32[4096,128]{1,0:T(8,128)S(1)} %bitcast.51, s32[4096]{0:T(1024)S(1)} %copy-done.22), kind=kCustom, calls=%fused_computation.2.clone | custom fusion | bytes 4210688 | tf_op jit(solution)/shard_map/jit(_take)/gather | solution.py:98
  470.8 3.8 fusion.13
  (153 shorter events, 77.8 us)
Async XLA Ops:
  7.2 9.3 %copy-start.13 = (bf16[128,4096]{1,0:T(8,128)(2,1)S(1)}, bf16[128,4096]{1,0:T(8,128)(2,1)}, u32[]{:S(2)}) copy-start(bf16[128,4096]{1,0:T(8,128)(2,1)} %param.15) | copy-start | bytes 3145732
  7.2 123.6 %all-gather.4.cloned.1.call-start = ((), (), s32[]{:S(2)}) async-start(), calls=%async_computation | async-start | bytes 4456448 | tf_op jit(solution)/shard_map/all_gather | solution.py:11
  13.8 0.9 copy-start.24
  13.8 8.8 %copy-start.20 = (s32[4096]{0:T(1024)}, s32[4096]{0:T(1024)S(1)}, u32[]{:S(2)}) copy-start(s32[4096]{0:T(1024)S(1)} %fusion.51) | copy-start | bytes 49156
  14.0 23.7 %copy-start.16 = (pred[256,16]{1,0:T(8,128)(4,1)}, pred[256,16]{1,0:T(8,128)(4,1)S(1)}, u32[]{:S(2)}) copy-start(pred[256,16]{1,0:T(8,128)(4,1)S(1)} %broadcast_in_dim.68) | copy-start | bytes 12292
  16.5 1.0 copy-start.4
  17.1 1.1 copy-start.6
  22.6 15.1 %copy-start.1 = (f32[256,16,128]{2,1,0:T(8,128)}, f32[256,16,128]{2,1,0:T(8,128)S(1)}, u32[]{:S(2)}) copy-start(f32[256,16,128]{2,1,0:T(8,128)S(1)} %rev.3) | copy-start | bytes 6291460
  42.2 3.1 copy-start.23
  42.2 9.8 %copy-start.28 = (f32[256,16]{0,1:T(8,128)S(1)}, f32[256,16]{0,1:T(8,128)}, u32[]{:S(2)}) copy-start(f32[256,16]{0,1:T(8,128)} %param.18) | copy-start | bytes 49156
  42.2 9.9 %copy-start.14 = (bf16[128,4096]{1,0:T(8,128)(2,1)S(1)}, bf16[128,4096]{1,0:T(8,128)(2,1)}, u32[]{:S(2)}) copy-start(bf16[128,4096]{1,0:T(8,128)(2,1)} %param.13) | copy-start | bytes 3145732
  42.2 11.2 %copy-start.15 = (bf16[128,4096]{1,0:T(8,128)(2,1)S(1)}, bf16[128,4096]{1,0:T(8,128)(2,1)}, u32[]{:S(2)}) copy-start(bf16[128,4096]{1,0:T(8,128)(2,1)} %param.16) | copy-start | bytes 3145732
  45.2 344.4 %all-gather.6.cloned.1.call-start = ((), (), s32[]{:S(2)}) async-start(), calls=%async_computation.1 | async-start | bytes 4456448 | tf_op jit(solution)/shard_map/all_gather | solution.py:11
  45.4 36.5 %copy-start.7 = (f32[256,16]{1,0:T(8,128)}, f32[256,16]{1,0:T(8,128)S(1)}, u32[]{:S(2)}) copy-start(f32[256,16]{1,0:T(8,128)S(1)} %copy.69) | copy-start | bytes 49156
  52.0 29.8 %copy-start.9 = (f32[256,16]{1,0:T(8,128)}, f32[256,16]{1,0:T(8,128)S(1)}, u32[]{:S(2)}) copy-start(f32[256,16]{1,0:T(8,128)S(1)} %copy.68) | copy-start | bytes 49156
  81.9 34.4 %copy-start.2 = (bf16[4096,128]{1,0:T(8,128)(2,1)S(1)}, bf16[4096,128]{1,0:T(8,128)(2,1)}, u32[]{:S(2)}) copy-start(bf16[4096,128]{1,0:T(8,128)(2,1)} %gather_fusion) | copy-start | bytes 3145732
  81.9 34.4 %copy-start.17 = (pred[256,16]{1,0:T(8,128)(4,1)S(1)}, pred[256,16]{1,0:T(8,128)(4,1)}, u32[]{:S(2)}) copy-start(pred[256,16]{1,0:T(8,128)(4,1)} %copy-done.16) | copy-start | bytes 12292
  110.6 5.7 %copy-start = (f32[256,128,128]{2,1,0:T(8,128)}, f32[256,128,128]{2,1,0:T(8,128)S(1)}, u32[]{:S(2)}) copy-start(f32[256,128,128]{2,1,0:T(8,128)S(1)} %fusion.22) | copy-start | bytes 50331652
  131.7 3.0 copy-start.10
  131.7 2.9 copy-start.12
  139.6 15.5 %copy-start.26 = (pred[4096]{0:T(1024)(128)(4,1)S(1)}, pred[4096]{0:T(1024)(128)(4,1)}, u32[]{:S(2)}) copy-start(pred[4096]{0:T(1024)(128)(4,1)} %compare_and_fusion) | copy-start | bytes 12292
  155.1 5.1 %copy-start.21 = (s32[4096]{0:T(1024)S(1)}, s32[4096]{0:T(1024)}, u32[]{:S(2)}) copy-start(s32[4096]{0:T(1024)} %copy-done.20) | copy-start | bytes 49156
  160.2 14.2 %copy-start.25 = (pred[4096]{0:T(1024)(128)(4,1)S(1)}, pred[4096]{0:T(1024)(128)(4,1)}, u32[]{:S(2)}) copy-start(pred[4096]{0:T(1024)(128)(4,1)} %copy-done.24) | copy-start | bytes 12292
  188.5 5.6 %copy-start.3 = (f32[16,4096]{1,0:T(8,128)S(1)}, f32[16,4096]{1,0:T(8,128)}, u32[]{:S(2)}) copy-start(f32[16,4096]{1,0:T(8,128)} %get-tuple-element.137) | copy-start | bytes 786436
  195.8 6.0 %copy-start.18 = (pred[256,16]{1,0:T(8,128)(4,1)S(1)}, pred[256,16]{1,0:T(8,128)(4,1)}, u32[]{:S(2)}) copy-start(pred[256,16]{1,0:T(8,128)(4,1)} %copy-done.16) | copy-start | bytes 12292
  201.8 13.9 %copy-start.8 = (f32[256,16]{1,0:T(8,128)S(1)}, f32[256,16]{1,0:T(8,128)}, u32[]{:S(2)}) copy-start(f32[256,16]{1,0:T(8,128)} %copy-done.7) | copy-start | bytes 49156
  215.7 26.9 %copy-start.19 = (f32[16,256]{0,1:T(8,128)S(1)}, f32[16,256]{0,1:T(8,128)}, u32[]{:S(2)}) copy-start(f32[16,256]{0,1:T(8,128)} %copy.77) | copy-start | bytes 49156
  449.5 2.0 copy-start.11
  451.4 5.1 %copy-start.22 = (s32[4096]{0:T(1024)S(1)}, s32[4096]{0:T(1024)}, u32[]{:S(2)}) copy-start(s32[4096]{0:T(1024)} %fusion.52) | copy-start | bytes 49156
  456.6 14.2 %copy-start.5 = (bf16[128,4096]{0,1:T(8,128)(2,1)S(1)}, bf16[128,4096]{0,1:T(8,128)(2,1)}, u32[]{:S(2)}) copy-start(bf16[128,4096]{0,1:T(8,128)(2,1)} %copy-done.4) | copy-start | bytes 3145732
  456.6 14.2 %copy-start.27 = (pred[4096]{0:T(1024)(128)(4,1)S(1)}, pred[4096]{0:T(1024)(128)(4,1)}, u32[]{:S(2)}) copy-start(pred[4096]{0:T(1024)(128)(4,1)} %compare_and_fusion) | copy-start | bytes 12292
Sparse Core Ops, SparseCore 0:
  45.3 53.8 all-gather.3
  186.4 116.4 all-gather.5
where the time goes:
time: 493 us; the launch traced here: 484 us
  blocking collectives  153 us (31%)
  local copies, waits for them, and re-layouts  144 us (29%)
  matrix products  121 us (25%)
  other arithmetic  49.6 us (10%)
  between operations  15.4 us (3%)
    psum x1, blocking collectives, on_device(): filter_grad = lax.psum(local_grad, 'ctx')  127 us
    dot_general x1, matrix products, on_device(): jnp.einsum('gmt,gms->gts', powers * residue[:, :, None], inverse_powers,...  28.7 us
    dot_general x1, matrix products, on_device(): inner = jnp.einsum('gts,gms->gmt', cross, inverse_powers, precision=high)  26.9 us
    all_gather x1, blocking collectives, carried_in(): gathered = jax.tree.map(lambda a: lax.all_gather(a, axis), part)  26 us
    reshape x15, local copies, waits for them, and re-layouts, chain_decays(): widened = jnp.repeat(later[0], per_group, axis=1)  23.4 us
    unnamed x69, local copies, waits for them, and re-layouts  19.9 us
    dot_general x1, matrix products, on_device(): jnp.einsum('gts,gct->gcs', toeplitz, upstream_sorted, precision=high)  17.6 us
    add x15, other arithmetic, chain_decays(): return (earlier[0] * later[0], widened * earlier[1] + later[1])  16.3 us
  transfers between devices with their start and end apart: 2, of which 0 were waited for; matrix products, arithmetic and copies ran while one was open for 27% of the time, Pallas kernels for 0%

commit v1 on v0

--- a/solution.py
+++ b/solution.py
@@ -2,6 +2,7 @@
 import jax.numpy as jnp
 from jax import lax
 from jax.sharding import PartitionSpec as P
+from jax.lax import all_gather
 
 
 def carried_in(part, axis, combine, identity, reverse):
@@ -92,7 +93,7 @@
         local_grad
         + jnp.sum((carry_in * head_term).reshape(mode_count, group_count, per_group), axis=2).T
     )
-    filter_grad = lax.psum(local_grad, "ctx")
+    filter_grad = all_gather(local_grad, axis_name="ctx").sum(axis=0)
     filter_update = filter_grad / jnp.sqrt(jnp.mean(filter_grad * filter_grad) + 1e-06)
     filtered = jnp.take(out_sorted.reshape(channel_count, row_count), inverse, axis=0).T
     mixed_grad = jnp.take(back_sorted.reshape(channel_count, row_count), inverse, axis=0).T

time: 493 us -> 462 us (0.937)
  blocking collectives: 153 us -> 121 us
    psum x1 -> x0, blocking collectives: 127 us -> none  [on_device(): filter_grad = lax.psum(local_grad, 'ctx')]
    all_gather x0 -> x1, blocking collectives: none -> 94.7 us  [on_device(): filter_grad = all_gather(local_grad, axis_name='ctx').sum(axis=0)]
  transfers between devices with their start and end apart: 2 -> 2, of which waited for: 0 -> 0; matrix products, arithmetic and copies ran while one was open for 27% -> 29% of each run, Pallas kernels for 0% -> 0%
where the time goes in v1:
time: 462 us; the launch traced here: 454 us
  local copies, waits for them, and re-layouts  144 us (31%)
  matrix products  122 us (26%)
  blocking collectives  121 us (26%)
  other arithmetic  51.4 us (11%)
  between operations  15.4 us (3%)
    all_gather x1, blocking collectives, on_device(): filter_grad = all_gather(local_grad, axis_name='ctx').sum(axis=0)  94.7 us
    dot_general x1, matrix products, on_device(): jnp.einsum('gmt,gms->gts', powers * residue[:, :, None], inverse_powers,...  28.7 us
    dot_general x1, matrix products, on_device(): inner = jnp.einsum('gts,gms->gmt', cross, inverse_powers, precision=high)  26.9 us
    all_gather x1, blocking collectives, carried_in(): gathered = jax.tree.map(lambda a: lax.all_gather(a, axis), part)  26 us
    reshape x15, local copies, waits for them, and re-layouts, chain_decays(): widened = jnp.repeat(later[0], per_group, axis=1)  23.4 us
    unnamed x69, local copies, waits for them, and re-layouts  19.9 us
    dot_general x1, matrix products, on_device(): jnp.einsum('gts,gct->gcs', toeplitz, upstream_sorted, precision=high)  17.8 us
    add x15, other arithmetic, chain_decays(): return (earlier[0] * later[0], widened * earlier[1] + later[1])  16.3 us
  transfers between devices with their start and end apart: 2, of which 0 were waited for; matrix products, arithmetic and copies ran while one was open for 29% of the time, Pallas kernels for 0%

profile of v1, /device:TPU:0, one launch (start us, length us, event | category | flops | bytes accessed | tf_op | source)
XLA Modules:
  0.0 453.6 jit_solution(8318456461130630483)
XLA Ops:
  7.2 6.6 %sort.31 = (s32[4096]{0:T(1024)}, s32[4096]{0:T(1024)S(1)}) sort(s32[4096]{0:T(1024)} %param.19, s32[4096]{0:T(1024)S(1)} %iota.26), dimensions={0}, to_apply=%region_0.0 | sort | flops 49152 | bytes 65536 | tf_op jit(solution)/shard_map/jit(argsort)/sort | solution.py:29
  19.9 2.7 rev.3
  22.7 15.0 %gather_fusion = bf16[4096,128]{1,0:T(8,128)(2,1)} fusion(bf16[4096,128]{1,0:T(8,128)(2,1)S(1)} %bitcast.53, s32[4096]{0:T(1024)S(1)} %fusion.51), kind=kCustom, calls=%fused_computation.3 | custom fusion | bytes 2113536 | tf_op jit(solution)/shard_map/jit(_take)/gather | solution.py:37
  37.7 4.5 fusion.47
  42.2 3.0 copy.87
  45.4 5.8 %sort.32 = (s32[4096]{0:T(1024)}, s32[4096]{0:T(1024)S(1)}) sort(s32[4096]{0:T(1024)S(1)} %get-tuple-element.136, s32[4096]{0:T(1024)S(1)} %iota.27), dimensions={0}, to_apply=%region_3.4 | sort | flops 49152 | bytes 65536 | tf_op jit(solution)/shard_map/jit(argsort)/sort | solution.py:30
  54.7 26.0 %all-gather = f32[256,256]{1,0:T(8,128)} all-gather(f32[16,256]{1,0:T(8,128)S(1)} %get-tuple-element.191), channel_id=2, replica_groups=mesh['groups'=2,'ctx'=16] {'ctx'}, dimensions={0}, use_global_device_ids=true | all-gather | bytes 278528 | tf_op jit(solution)/shard_map/all_gather | solution.py:12
  81.9 28.7 %fusion.22 = f32[256,128,128]{2,1,0:T(8,128)S(1)} fusion(f32[256,16]{1,0:T(8,128)S(1)} %copy.86, f32[256,16]{1,0:T(8,128)S(1)} %copy.85, f32[256,16]{1,0:T(8,128)S(1)} %copy.84), kind=kOutput, calls=%fused_computation.38 | convolution fusion | flops 806879232 | bytes 16826368 | tf_op jit(solution)/shard_map/gmt,gms->gts/dot_general | solution.py:54
  110.6 5.7 %copy-done = f32[256,128,128]{2,1,0:T(8,128)} copy-done((f32[256,128,128]{2,1,0:T(8,128)}, f32[256,128,128]{2,1,0:T(8,128)S(1)}, u32[]{:S(2)}) %copy-start) | copy-done | bytes 16777240
  116.3 14.5 %fusion.4 = f32[256,16,128]{2,1,0:T(8,128)} fusion(f32[256,128,128]{2,1,0:T(8,128)S(1)} %fusion.22, pred[128,128]{1,0:T(8,128)(4,1)S(1)} %iota_compare_fusion, bf16[256,16,128]{2,1,0:T(8,128)(2,1)S(1)} %bitcast.60, pred[256,16]{1,0:T(8,128)(4,1)S(1)} %copy-done.17), kind=kOutput, calls=%fused_computation.12 | convolution fusion | flops 810024960 | bytes 19943424 | tf_op jit(solution)/shard_map/gts,gcs->gct/dot_general | solution.py:58
  131.7 2.9 copy.100
  134.6 5.0 %fusion.28 = f32[256,16,128]{2,1,0:T(8,128)S(1)} fusion(f32[256,16,128]{2,1,0:T(8,128)} %fusion.4, f32[16,256,16]{0,2,1:T(8,128)} %bitcast.62, f32[256,16]{1,0:T(8,128)S(1)} %copy-done.12, f32[256,16]{1,0:T(8,128)S(1)} %copy-done.10, f32[256,16]{1,0:T(8,128)S(1)} %copy.84), kind=kOutput, calls=%fused_computation.43 | convolution fusion | flops 102760448 | bytes 4505600 | tf_op jit(solution)/shard_map/gmt,mgc->gct/dot_general | solution.py:84
  139.6 15.5 %gather_fusion.1 = f32[4096,128]{1,0:T(8,128)} fusion(f32[4096,128]{1,0:T(8,128)S(1)} %bitcast.51, s32[4096]{0:T(1024)} %fusion.52), kind=kCustom, calls=%fused_computation.clone | custom fusion | bytes 4210688 | tf_op jit(solution)/shard_map/jit(_take)/gather | solution.py:98
  155.1 5.1 %fusion.16 = (bf16[128,4096]{0,1:T(8,128)(2,1)}, bf16[128,4096]{0,1:T(8,128)(2,1)}, f32[4096,128]{1,0:T(8,128)S(1)}) fusion(bf16[128,4096]{0,1:T(8,128)(2,1)} %copy.90, f32[4096,128]{1,0:T(8,128)} %gather_fusion.1, pred[4096]{0:T(1024)(128)(4,1)S(1)} %copy-done.26, bf16[128,4096]{0,1:T(8,128)(2,1)} %copy.81), kind=kLoop, calls=%fused_computation.30 | loop fusion | flops 4194304 | bytes 8392704 | tf_op jit(solution)/shard_map/convert_element_type | solution.py:101
  160.2 14.2 %gather_fusion.2 = f32[4096,128]{1,0:T(8,128)} fusion(f32[4096,128]{1,0:T(8,128)S(1)} %get-tuple-element.189, s32[4096]{0:T(1024)S(1)} %copy-done.21), kind=kCustom, calls=%fused_computation.1.clone | custom fusion | bytes 4210688 | tf_op jit(solution)/shard_map/jit(_take)/gather | solution.py:42
  174.4 3.6 broadcast_select_fusion
  178.0 5.4 %fusion.25 = f32[256,16,16]{2,1,0:T(8,128)} fusion(f32[256,16,128]{2,1,0:T(8,128)S(1)} %bitcast.54, f32[256,16]{1,0:T(8,128)S(1)} %copy-done.12, f32[256,16]{1,0:T(8,128)S(1)} %copy.84), kind=kOutput, calls=%fused_computation.42 | convolution fusion | flops 101711872 | bytes 2392064 | tf_op jit(solution)/shard_map/gmt,gct->mgc/dot_general | solution.py:63
  183.4 2.9 copy.91
  186.3 2.3 copy.96
  188.5 2.7 copy.95
  191.2 2.9 copy.93
  195.8 3.0 reshape.82
  198.8 2.2 reduce_sum.37
  201.8 13.9 %fusion.46 = f32[256,128,128]{2,1,0:T(8,128)S(1)} fusion(f32[256,16,128]{2,1,0:T(8,128)S(1)} %bitcast.55, bf16[256,16,128]{2,1,0:T(8,128)(2,1)S(1)} %bitcast.61, pred[256,16]{1,0:T(8,128)(4,1)S(1)} %copy-done.18), kind=kOutput, calls=%fused_computation.57 | convolution fusion | flops 805830656 | bytes 19927040 | tf_op jit(solution)/shard_map/gct,gcs->gts/dot_general | solution.py:88
  215.7 26.9 %multiply_reduce_fusion = f32[256,16]{1,0:T(8,128)S(1)} fusion(f32[256,16]{1,0:T(8,128)S(1)} %copy.84, f32[256,128,128]{2,1,0:T(8,128)S(1)} %fusion.46, pred[128,128]{1,0:T(8,128)(4,1)S(1)} %iota_compare_fusion, f32[256,16]{1,0:T(8,128)S(1)} %copy-done.8), kind=kOutput, calls=%fused_computation.32 | convolution fusion | flops 811593728 | bytes 16842752 | tf_op jit(solution)/shard_map/gts,gms->gmt/dot_general | solution.py:90
  242.6 94.7 %all-gather.1 = f32[4096,16]{1,0:T(8,128)} all-gather(f32[256,16]{1,0:T(8,128)S(1)} %bitcast_add_fusion.2), channel_id=3, replica_groups=mesh['groups'=2,'ctx'=16] {'ctx'}, dimensions={0}, use_global_device_ids=true | all-gather | bytes 278528 | tf_op jit(solution)/shard_map/all_gather | solution.py:96
  341.2 17.8 %fusion.2 = f32[256,16,128]{2,1,0:T(8,128)} fusion(f32[256,16,128]{2,1,0:T(8,128)S(1)} %bitcast.56, f32[256,128,128]{2,1,0:T(8,128)} %copy-done, pred[128,128]{1,0:T(8,128)(4,1)S(1)} %iota_compare_fusion), kind=kOutput, calls=%fused_computation.10 | convolution fusion | flops 809500672 | bytes 20987904 | tf_op jit(solution)/shard_map/gts,gct->gcs/dot_general | solution.py:59
  359.0 59.8 %while.27 = (s32[]{:T(128)}, f32[16,4096]{1,0:T(8,128)S(1)}, s32[]{:T(128)}, f32[16,16,256]{2,1,0:T(8,128)}, f32[16,16,4096]{2,1,0:T(8,128)}, /*index=5*/s32[]{:T(128)}, s32[]{:T(128)}, s32[]{:T(128)}, s32[]{:T(128)}) while((s32[]{:T(128)}, f32[16,4096]{1,0:T(8,128)S(1)}, s32[]{:T(128)}, f32[16,16,256]{2,1,0:T(8,128)}, ...), condition=%wide.region_5.7_spmd, body=%wide.region_4.6_spmd.sunk | while | flops 131078 | bytes 1884315 | solution.py:21
  418.8 1.9 copy.101
  420.7 5.1 %fusion.31 = f32[256,16,128]{2,1,0:T(8,128)S(1)} fusion(f32[256,16,128]{2,1,0:T(8,128)} %fusion.2, f32[16,256,16]{0,2,1:T(8,128)} %bitcast.65, f32[256,16,128]{2,1,0:T(8,128)} %copy-done.1, f32[256,16]{1,0:T(8,128)S(1)} %copy-done.11), kind=kOutput, calls=%fused_computation.44 | convolution fusion | flops 101711872 | bytes 6569984 | tf_op jit(solution)/shard_map/gms,mgc->gcs/dot_general | solution.py:85
  425.9 14.2 %gather_fusion.3 = f32[4096,128]{1,0:T(8,128)} fusion(f32[4096,128]{1,0:T(8,128)S(1)} %bitcast.52, s32[4096]{0:T(1024)S(1)} %copy-done.22), kind=kCustom, calls=%fused_computation.2.clone | custom fusion | bytes 4210688 | tf_op jit(solution)/shard_map/jit(_take)/gather | solution.py:99
  440.1 3.8 fusion.13
  (154 shorter events, 79.5 us)
Async XLA Ops:
  7.2 9.3 %copy-start.13 = (bf16[128,4096]{1,0:T(8,128)(2,1)S(1)}, bf16[128,4096]{1,0:T(8,128)(2,1)}, u32[]{:S(2)}) copy-start(bf16[128,4096]{1,0:T(8,128)(2,1)} %param.15) | copy-start | bytes 3145732
  7.2 123.6 %all-gather.5.cloned.1.call-start = ((), (), s32[]{:S(2)}) async-start(), calls=%async_computation | async-start | bytes 4456448 | tf_op jit(solution)/shard_map/all_gather | solution.py:12
  13.8 0.9 copy-start.24
  13.8 8.8 %copy-start.20 = (s32[4096]{0:T(1024)}, s32[4096]{0:T(1024)S(1)}, u32[]{:S(2)}) copy-start(s32[4096]{0:T(1024)S(1)} %fusion.51) | copy-start | bytes 49156
  14.0 23.7 %copy-start.16 = (pred[256,16]{1,0:T(8,128)(4,1)}, pred[256,16]{1,0:T(8,128)(4,1)S(1)}, u32[]{:S(2)}) copy-start(pred[256,16]{1,0:T(8,128)(4,1)S(1)} %broadcast_in_dim.68) | copy-start | bytes 12292
  16.5 1.0 copy-start.4
  17.1 1.1 copy-start.6
  22.6 15.1 %copy-start.1 = (f32[256,16,128]{2,1,0:T(8,128)}, f32[256,16,128]{2,1,0:T(8,128)S(1)}, u32[]{:S(2)}) copy-start(f32[256,16,128]{2,1,0:T(8,128)S(1)} %rev.3) | copy-start | bytes 6291460
  42.2 3.1 copy-start.23
  42.2 9.8 %copy-start.28 = (f32[256,16]{0,1:T(8,128)S(1)}, f32[256,16]{0,1:T(8,128)}, u32[]{:S(2)}) copy-start(f32[256,16]{0,1:T(8,128)} %param.18) | copy-start | bytes 49156
  42.2 9.9 %copy-start.14 = (bf16[128,4096]{1,0:T(8,128)(2,1)S(1)}, bf16[128,4096]{1,0:T(8,128)(2,1)}, u32[]{:S(2)}) copy-start(bf16[128,4096]{1,0:T(8,128)(2,1)} %param.13) | copy-start | bytes 3145732
  42.2 11.2 %copy-start.15 = (bf16[128,4096]{1,0:T(8,128)(2,1)S(1)}, bf16[128,4096]{1,0:T(8,128)(2,1)}, u32[]{:S(2)}) copy-start(bf16[128,4096]{1,0:T(8,128)(2,1)} %param.16) | copy-start | bytes 3145732
  45.2 313.7 %all-gather.7.cloned.1.call-start = ((), (), s32[]{:S(2)}) async-start(), calls=%async_computation.1 | async-start | bytes 4456448 | tf_op jit(solution)/shard_map/all_gather | solution.py:12
  45.4 36.5 %copy-start.7 = (f32[256,16]{1,0:T(8,128)}, f32[256,16]{1,0:T(8,128)S(1)}, u32[]{:S(2)}) copy-start(f32[256,16]{1,0:T(8,128)S(1)} %copy.86) | copy-start | bytes 49156
  52.0 29.8 %copy-start.9 = (f32[256,16]{1,0:T(8,128)}, f32[256,16]{1,0:T(8,128)S(1)}, u32[]{:S(2)}) copy-start(f32[256,16]{1,0:T(8,128)S(1)} %copy.85) | copy-start | bytes 49156
  81.9 34.4 %copy-start.2 = (bf16[4096,128]{1,0:T(8,128)(2,1)S(1)}, bf16[4096,128]{1,0:T(8,128)(2,1)}, u32[]{:S(2)}) copy-start(bf16[4096,128]{1,0:T(8,128)(2,1)} %gather_fusion) | copy-start | bytes 3145732
  81.9 34.4 %copy-start.17 = (pred[256,16]{1,0:T(8,128)(4,1)S(1)}, pred[256,16]{1,0:T(8,128)(4,1)}, u32[]{:S(2)}) copy-start(pred[256,16]{1,0:T(8,128)(4,1)} %copy-done.16) | copy-start | bytes 12292
  110.6 5.7 %copy-start = (f32[256,128,128]{2,1,0:T(8,128)}, f32[256,128,128]{2,1,0:T(8,128)S(1)}, u32[]{:S(2)}) copy-start(f32[256,128,128]{2,1,0:T(8,128)S(1)} %fusion.22) | copy-start | bytes 50331652
  131.7 3.0 copy-start.10
  131.7 2.9 copy-start.12
  139.6 15.5 %copy-start.26 = (pred[4096]{0:T(1024)(128)(4,1)S(1)}, pred[4096]{0:T(1024)(128)(4,1)}, u32[]{:S(2)}) copy-start(pred[4096]{0:T(1024)(128)(4,1)} %compare_and_fusion) | copy-start | bytes 12292
  155.1 5.1 %copy-start.21 = (s32[4096]{0:T(1024)S(1)}, s32[4096]{0:T(1024)}, u32[]{:S(2)}) copy-start(s32[4096]{0:T(1024)} %copy-done.20) | copy-start | bytes 49156
  160.2 14.2 %copy-start.25 = (pred[4096]{0:T(1024)(128)(4,1)S(1)}, pred[4096]{0:T(1024)(128)(4,1)}, u32[]{:S(2)}) copy-start(pred[4096]{0:T(1024)(128)(4,1)} %copy-done.24) | copy-start | bytes 12292
  188.5 5.6 %copy-start.3 = (f32[16,4096]{1,0:T(8,128)S(1)}, f32[16,4096]{1,0:T(8,128)}, u32[]{:S(2)}) copy-start(f32[16,4096]{1,0:T(8,128)} %get-tuple-element.137) | copy-start | bytes 786436
  195.8 6.0 %copy-start.18 = (pred[256,16]{1,0:T(8,128)(4,1)S(1)}, pred[256,16]{1,0:T(8,128)(4,1)}, u32[]{:S(2)}) copy-start(pred[256,16]{1,0:T(8,128)(4,1)} %copy-done.16) | copy-start | bytes 12292
  201.8 13.9 %copy-start.8 = (f32[256,16]{1,0:T(8,128)S(1)}, f32[256,16]{1,0:T(8,128)}, u32[]{:S(2)}) copy-start(f32[256,16]{1,0:T(8,128)} %copy-done.7) | copy-start | bytes 49156
  215.7 26.9 %copy-start.19 = (f32[16,256]{0,1:T(8,128)S(1)}, f32[16,256]{0,1:T(8,128)}, u32[]{:S(2)}) copy-start(f32[16,256]{0,1:T(8,128)} %copy.94) | copy-start | bytes 49156
  418.8 2.0 copy-start.11
  420.7 5.1 %copy-start.22 = (s32[4096]{0:T(1024)S(1)}, s32[4096]{0:T(1024)}, u32[]{:S(2)}) copy-start(s32[4096]{0:T(1024)} %fusion.52) | copy-start | bytes 49156
  425.9 14.2 %copy-start.5 = (bf16[128,4096]{0,1:T(8,128)(2,1)S(1)}, bf16[128,4096]{0,1:T(8,128)(2,1)}, u32[]{:S(2)}) copy-start(bf16[128,4096]{0,1:T(8,128)(2,1)} %copy-done.4) | copy-start | bytes 3145732
  425.9 14.2 %copy-start.27 = (pred[4096]{0:T(1024)(128)(4,1)S(1)}, pred[4096]{0:T(1024)(128)(4,1)}, u32[]{:S(2)}) copy-start(pred[4096]{0:T(1024)(128)(4,1)} %compare_and_fusion) | copy-start | bytes 12292
Sparse Core Ops, SparseCore 0:
  45.3 53.8 all-gather.4
  186.4 118.6 all-gather.6
